TPU v7x, 32 devices: a whole 2x2x4 slice. The times are simulated.
32 devices in a mesh: chan: 8 (over z, y), tm: 4 (over x, core).
Axes of the slice: x: 2, y: 2, z: 4, core: 2. Of those that a mesh axis runs over, the one named last changes fastest.
Arguments:
- records: float32 [4, 3200, 512], P('tm', 'chan'), may hold values from -6 to 6
- chan_order: int32 [512], replicated, may hold values from 0 to 511, each once
- live_mask: int32 [512], replicated, may hold values 0 or 1
Outputs:
- stacks: float32 [2, 512, 64, 128], P(None, 'chan', 'tm')
Inputs may be any that keep to these rules, and one draw needn't show every extreme that they name: chan_order holds every channel number once.
All inputs are finite; a program needn't handle non-finite values.
Results may differ from a plain program's by a relative error of at most 0.0041.
Values may be sent and summed in bfloat16 or wider, within the bound.
No kernel may reach another device: no remote copies, remote signals or barrier semaphores. Data moves between devices by JAX's collectives and lax.ppermute only.
A program may use at most 64 MiB of HBM per device.

v0:
```python
import math
import jax
import jax.numpy as jnp
from jax import lax
from jax.sharding import PartitionSpec as P

L = 200
FB = 101
NLAG = 128
ROUNDS = 2
WIN_TM = 16


def shifted(block, axis, distance):
    devices = range(lax.axis_size(axis))
    route = [((i - distance) % len(devices), i) for i in devices]
    return lax.ppermute(block, axis, route)


def forward_table():
    sample_index = jnp.arange(L, dtype=jnp.int32)
    freq_index = jnp.arange(FB, dtype=jnp.int32)
    phase_step = jnp.mod(sample_index[:, None] * freq_index[None, :], L)
    phase_angle = phase_step.astype(jnp.float32) * (2.0 * math.pi / L)
    return jnp.concatenate([jnp.cos(phase_angle), -jnp.sin(phase_angle)], axis=1)


def smoothing_table():
    freq_index = jnp.arange(FB, dtype=jnp.int32)
    nearby = (jnp.abs(freq_index[:, None] - freq_index[None, :]) <= 2).astype(jnp.float32)
    return nearby / jnp.sum(nearby, axis=0, keepdims=True)


def inverse_table():
    freq_index = jnp.arange(FB, dtype=jnp.int32)
    lag_index = jnp.arange(NLAG, dtype=jnp.int32) - NLAG // 2
    phase_step = jnp.mod(freq_index[:, None] * lag_index[None, :], L)
    phase_angle = phase_step.astype(jnp.float32) * (2.0 * math.pi / L)
    edge = (freq_index == 0) | (freq_index == L // 2)
    fold_weight = jnp.where(edge, 1.0, 2.0).astype(jnp.float32) / L
    return jnp.stack(
        [fold_weight[:, None] * jnp.cos(phase_angle), -fold_weight[:, None] * jnp.sin(phase_angle)]
    )


def whiten_spectra(windows, live_block, precision=lax.Precision.HIGHEST):
    window_mean = jnp.mean(windows, axis=-2, keepdims=True)
    centred = windows - window_mean
    normed = centred / jnp.sqrt(jnp.mean(centred * centred, axis=-2, keepdims=True) + 1e-05)
    spectrum = jnp.einsum("...lk,lg->...kg", normed, forward_table(), precision=precision)
    real_part = spectrum[..., :FB]
    imag_part = spectrum[..., FB:]
    power = real_part * real_part + imag_part * imag_part
    smoothed = jnp.einsum("...f,fg->...g", power, smoothing_table(), precision=precision)
    mean_power = jnp.mean(power, axis=-1, keepdims=True)
    scale = live_block.astype(jnp.float32)[:, None] / jnp.sqrt(smoothed + 0.1 * mean_power + 1e-05)
    return jnp.concatenate([real_part * scale, imag_part * scale], axis=-1).astype(jnp.bfloat16)


def correlate(partner, own_spec, inverse):
    partner = partner.reshape(partner.shape[0], partner.shape[1], 2, FB)
    own_spec = own_spec.reshape(own_spec.shape[0], own_spec.shape[1], 2, FB)
    rotated = jnp.concatenate([own_spec[:, :, 1:2], -own_spec[:, :, 0:1]], axis=2)
    real_sum = jnp.einsum("wicf,wjcf->fji", partner, own_spec, preferred_element_type=jnp.float32)
    imag_sum = jnp.einsum("wicf,wjcf->fji", partner, rotated, preferred_element_type=jnp.float32)
    return jnp.einsum(
        "cfji,cfl->jil", jnp.stack([real_sum, imag_sum]), inverse, precision=lax.Precision.HIGHEST
    )


def on_device_reduce(records, chan_order, live_mask):
    chan_count = lax.axis_size("chan")
    position = lax.axis_index("chan")
    blocked = jnp.take(records, chan_order, axis=2)
    own_block = lax.all_to_all(blocked, "chan", split_axis=2, concat_axis=1, tiled=True)
    block_width = own_block.shape[2]
    own_windows = own_block.reshape(WIN_TM, L, block_width)
    live_blocks = jnp.take(live_mask, chan_order).reshape(chan_count, block_width)
    own_live = lax.dynamic_index_in_dim(live_blocks, position, 0, keepdims=False)
    own_spectra = whiten_spectra(own_windows, own_live)
    inverse = inverse_table()
    results = []
    for round_index in range(ROUNDS):
        offset = max(1, round_index * chan_count // 4)
        partner_block = shifted(own_windows, "chan", offset)
        source = jnp.mod(position - offset, chan_count)
        partner_live = lax.dynamic_index_in_dim(live_blocks, source, 0, keepdims=False)
        partner = whiten_spectra(partner_block, partner_live)
        lagged = correlate(partner, own_spectra, inverse)
        lagged = lax.psum_scatter(lagged, "tm", scatter_dimension=1, tiled=True)
        results.append(lagged)
    return jnp.stack(results)


def on_device_local(records, chan_order, live_mask):
    chan_count = lax.axis_size("chan")
    tm_count = lax.axis_size("tm")
    tm_position = lax.axis_index("tm")
    samples, channels = (records.shape[1], records.shape[2])
    block_width = channels // chan_count
    slice_width = block_width // tm_count
    windows = records.reshape(samples // L, L, channels)
    spectra = whiten_spectra(windows, live_mask, precision=lax.Precision.HIGH)
    spectra = jnp.take(spectra, chan_order, axis=1)
    own = lax.all_to_all(spectra, "chan", split_axis=1, concat_axis=0, tiled=True)
    gathered = lax.all_gather(own, "tm", axis=0, tiled=True)
    windows_all = gathered.shape[0]
    own_spec = gathered.reshape(windows_all, block_width, 2, FB)
    rotated = jnp.concatenate([own_spec[:, :, 1:2], -own_spec[:, :, 0:1]], axis=2)
    both = jnp.concatenate([own_spec, rotated], axis=1)
    my_slice = lax.dynamic_slice_in_dim(gathered, tm_position * slice_width, slice_width, axis=1)
    partners = []
    for round_index in range(ROUNDS):
        offset = max(1, round_index * chan_count // 4)
        partners.append(shifted(my_slice, "chan", offset))
    partner = jnp.concatenate(partners, axis=1).reshape(windows_all, ROUNDS * slice_width, 2, FB)
    sums = jnp.einsum("wicf,wjcf->fji", partner, both, preferred_element_type=jnp.float32)
    sums = sums.reshape(FB, 2, block_width, ROUNDS, slice_width)
    lagged = jnp.einsum("fcjri,cfl->rjil", sums, inverse_table(), precision=lax.Precision.HIGH)
    return lagged


def on_device(records, chan_order, live_mask):
    samples = records.shape[1]
    channels = records.shape[2]
    chan_count = lax.axis_size("chan")
    tm_count = lax.axis_size("tm")
    local_ok = (
        samples % L == 0
        and channels % chan_count == 0
        and (channels // chan_count % tm_count == 0)
        and (samples // L * chan_count == WIN_TM)
    )
    if local_ok:
        return on_device_local(records, chan_order, live_mask)
    return on_device_reduce(records, chan_order, live_mask)


def solution(mesh):
    placed = (P("tm", "chan", None), P(), P())
    return jax.shard_map(
        on_device,
        mesh=mesh,
        in_specs=placed,
        out_specs=P(None, "chan", "tm", None),
        check_vma=False,
    )
```

profile of v0, /device:TPU:4, one launch (start us, length us, event | category | flops | bytes accessed | tf_op | source)
XLA Modules:
  0.0 117.0 jit_solution(12994349782055250445)
XLA Ops:
  6.5 0.0 all-gather.2.cloned.1.call-start
  6.5 0.4 sine_negate_fusion
  7.0 0.1 convert_reduce_fusion
  7.1 0.7 compare_select_fusion
  7.8 0.7 compare_and_fusion
  8.5 1.2 %reduce_sum.36 = f32[2,512]{1,0:T(2,128)S(1)} reduce(f32[2,200,512]{2,1,0:T(8,128)} %bitcast.33, f32[]{:T(128)} %constant.41.clone.1), dimensions={1}, to_apply=%region_0.0 | reduce | flops 203776 | bytes 823300 | tf_op jit(solution)/shard_map/reduce_sum | solution.py:47
  9.7 1.3 %multiply_reduce_fusion = f32[2,512]{1,0:T(2,128)S(1)} fusion(f32[2,200,512]{2,1,0:T(8,128)} %bitcast.34, f32[2,512]{1,0:T(2,128)S(1)} %broadcast_multiply_fusion.1), kind=kLoop, calls=%fused_computation.18 | loop fusion | flops 613376 | bytes 827392 | tf_op jit(solution)/shard_map/reduce_sum | solution.py:49
  11.0 0.0 copy-start
  11.0 1.8 %fusion.12 = f32[2,512,202]{1,2,0:T(8,128)S(1)} fusion(f32[2,200,512]{2,1,0:T(8,128)} %bitcast.35, f32[2,512]{1,0:T(2,128)S(1)} %add_sqrt_fusion, f32[2,512]{1,0:T(2,128)S(1)} %broadcast_multiply_fusion.1, f32[200,101]{1,0:T(8,128)S(1)} %get-tuple-element.11, f32[200,101]{1,0:T(8,128)S(1)} %get-tuple-element.12), kind=kOutput, calls=%fused_computation.16 | convolution fusion | flops 248667600 | bytes 1816384 | tf_op jit(solution)/shard_map/...lk,lg->...kg/dot_general | solution.py:50
  12.8 0.1 fusion.28
  12.9 0.0 copy-done
  12.9 0.5 multiply_convert_fusion.1
  13.4 0.1 pad_maximum_fusion.1
  13.5 0.4 copy.16
  14.0 2.6 %gather_fusion = bf16[512,2,202]{2,1,0:T(2,128)(2,1)S(1)} fusion(bf16[2,512,202]{2,0,1:T(2,128)(2,1)S(1)} %copy.16, s32[1024]{0:T(1024)S(1)} %pad_clamp_fusion), kind=kCustom, calls=%fused_computation | custom fusion | bytes 829440 | tf_op jit(solution)/shard_map/jit(_take)/gather | solution.py:104
  16.5 1.8 %fusion.15 = bf16[2,512,202]{2,0,1:T(2,128)(2,1)S(1)} fusion(bf16[512,2,202]{2,1,0:T(2,128)(2,1)S(1)} %gather_fusion, pred[512]{0:T(512)(128)(4,1)S(1)} %compare_and_fusion), kind=kLoop, calls=%fused_computation.20 | loop fusion | flops 206848 | bytes 827904 | tf_op jit(solution)/shard_map/jit(_take)/select_n | solution.py:104
  18.4 20.1 %all_to_all.18 = bf16[2,512,202]{2,0,1:T(2,128)(2,1)S(1)} all-to-all(bf16[2,512,202]{2,0,1:T(2,128)(2,1)S(1)} %fusion.15), channel_id=1, replica_groups=mesh['chan'=8,'tm'=4] {'chan'}, dimensions={1} | all-to-all | bytes 827392 | tf_op jit(solution)/shard_map/all_to_all | solution.py:105
  38.4 0.1 copy.17
  38.5 0.8 copy.18
  39.3 0.0 all-gather.2.cloned.1.call-update
  39.4 21.7 %all-gather.2.cloned.1.call-done = bf16[64,64,202]{2,1,0:T(8,128)(2,1)} async-done(((bf16[16,64,202]{2,1,0:T(8,128)(2,1)}), bf16[64,64,202]{2,1,0:T(8,128)(2,1)}) %all-gather.2.cloned.1.call-update) | async-done | bytes 1654800 | tf_op jit(solution)/shard_map/all_gather | solution.py:106
  61.1 1.9 %constant_dynamic-slice_fusion = bf16[64,16,202]{2,1,0:T(8,128)(2,1)} fusion(bf16[64,64,202]{2,1,0:T(8,128)(2,1)} %all-gather.2.cloned.1.call-done, s32[]{:T(128)S(6)} %select_n.58), kind=kLoop, calls=%fused_computation.67 | loop fusion | bytes 827396 | tf_op jit(solution)/shard_map/dynamic_slice | solution.py:111
  63.0 1.5 %collective-permute-start = (bf16[64,16,202]{2,1,0:T(8,128)(2,1)}, bf16[64,16,202]{2,1,0:T(8,128)(2,1)}, u32[]{:S(2)}, u32[]{:S(2)}) collective-permute-start(bf16[64,16,202]{2,1,0:T(8,128)(2,1)} %constant_dynamic-slice_fusion), channel_id=1, source_target_pairs={{28,0},{0,4},{4,8},{8,12},{12,16},{16,20},{20,24},{24,28},{29,1},{... | collective-permute-start | bytes 1241096 | tf_op jit(solution)/shard_map/ppermute | solution.py:17
  64.5 1.5 %collective-permute-start.1 = (bf16[64,16,202]{2,1,0:T(8,128)(2,1)}, bf16[64,16,202]{2,1,0:T(8,128)(2,1)}, u32[]{:S(2)}, u32[]{:S(2)}) collective-permute-start(bf16[64,16,202]{2,1,0:T(8,128)(2,1)} %constant_dynamic-slice_fusion), channel_id=1, source_target_pairs={{24,0},{28,4},{0,8},{4,12},{8,16},{12,20},{16,24},{20,28},{25,1},{... | collective-permute-start | bytes 1241096 | tf_op jit(solution)/shard_map/ppermute | solution.py:17
  66.0 0.2 cosine_multiply_fusion
  66.2 4.3 %reshape.185 = bf16[64,64,2,101]{3,2,1,0:T(2,128)(2,1)} reshape(bf16[64,64,202]{2,1,0:T(8,128)(2,1)} %all-gather.2.cloned.1.call-done) | data formatting | bytes 3309568 | tf_op jit(solution)/shard_map/reshape | solution.py:108
  70.5 6.4 %copy.21 = bf16[64,64,2,101]{1,0,2,3:T(8,128)(2,1)S(1)} copy(bf16[64,64,2,101]{3,2,1,0:T(2,128)(2,1)} %reshape.185) | data formatting | bytes 3309568 | tf_op jit(solution)/shard_map/reshape | solution.py:108
  76.9 2.0 %fusion.44 = (bf16[64,64,1,101]{1,0,2,3:T(8,128)(2,1)}, bf16[64,64,1,101]{1,0,2,3:T(8,128)(2,1)}) fusion(bf16[64,64,2,101]{1,0,2,3:T(8,128)(2,1)S(1)} %copy.21), kind=kLoop, calls=%fused_computation.73 | loop fusion | flops 413696 | bytes 3309568 | tf_op jit(solution)/shard_map/slice | solution.py:109
  79.0 0.0 collective-permute-done
  79.0 11.4 %collective-permute-done.1 = bf16[64,16,202]{2,1,0:T(8,128)(2,1)} collective-permute-done((bf16[64,16,202]{2,1,0:T(8,128)(2,1)}, bf16[64,16,202]{2,1,0:T(8,128)(2,1)}, u32[]{:S(2)}, u32[]{:S(2)}) %collective-permute-start.1) | collective-permute-done | bytes 413728 | tf_op jit(solution)/shard_map/ppermute | solution.py:17
  90.4 2.4 %pad_maximum_fusion = bf16[64,32,202]{2,1,0:T(8,128)(2,1)} fusion(bf16[64,16,202]{2,1,0:T(8,128)(2,1)} %collective-permute-done.1, bf16[64,16,202]{2,1,0:T(8,128)(2,1)} %collective-permute-done), kind=kLoop, calls=%fused_computation.14 | loop fusion | flops 1654784 | bytes 1654784 | tf_op jit(solution)/shard_map/concatenate | solution.py:116
  92.8 2.5 %reshape.186 = bf16[64,32,2,101]{3,2,1,0:T(2,128)(2,1)} reshape(bf16[64,32,202]{2,1,0:T(8,128)(2,1)} %pad_maximum_fusion) | data formatting | bytes 1654784 | tf_op jit(solution)/shard_map/reshape | solution.py:116
  95.3 4.5 %copy.22 = bf16[64,32,2,101]{0,1,2,3:T(8,128)(2,1)} copy(bf16[64,32,2,101]{3,2,1,0:T(2,128)(2,1)} %reshape.186) | data formatting | bytes 1654784 | tf_op jit(solution)/shard_map/reshape | solution.py:116
  99.8 5.8 %fusion.6 = f32[101,128,32]{1,2,0:T(8,128)} fusion(bf16[64,32,2,101]{0,1,2,3:T(8,128)(2,1)} %copy.22, bf16[64,64,1,101]{1,0,2,3:T(8,128)(2,1)} %get-tuple-element.6, bf16[64,64,1,101]{1,0,2,3:T(8,128)(2,1)} %get-tuple-element.5, bf16[64,64,2,101]{1,0,2,3:T(8,128)(2,1)S(1)} %copy.21), kind=kOutput, calls=%fused_computation.8 | convolution fusion | flops 115834880 | bytes 5791744 | tf_op jit(solution)/shard_map/wicf,wjcf->fji/dot_general | solution.py:117
  105.6 1.9 %copy.29 = f32[101,128,32]{0,1,2:T(8,128)S(1)} copy(f32[101,128,32]{1,2,0:T(8,128)} %fusion.6) | data formatting | bytes 3309568 | tf_op jit(solution)/shard_map/reshape | solution.py:118
  107.5 1.0 convolution_bitcast_fusion
  108.5 1.6 %copy.25 = f32[2,64,16,128]{3,2,1,0:T(8,128)} copy(f32[2,64,16,128]{3,1,2,0:T(8,128)S(1)} %convolution_bitcast_fusion) | data formatting | bytes 2097152 | tf_op jit(solution)/shard_map/fcjri,cfl->rjil/transpose | solution.py:119
  (7 shorter events, 0.0 us)
Async XLA Ops:
  6.5 54.6 %all-gather.2.cloned.1.call-start = ((), (), s32[]{:S(2)}) async-start(), calls=%async_computation.1 | async-start | bytes 2621440 | tf_op jit(solution)/shard_map/all_gather | solution.py:106
  11.0 1.9 %copy-start = (s32[512]{0:T(512)S(1)}, s32[512]{0:T(512)}, u32[]{:S(2)}) copy-start(s32[512]{0:T(512)} %param.5) | copy-start | bytes 6148
  63.0 16.0 %collective-permute-start = (bf16[64,16,202]{2,1,0:T(8,128)(2,1)}, bf16[64,16,202]{2,1,0:T(8,128)(2,1)}, u32[]{:S(2)}, u32[]{:S(2)}) collective-permute-start(bf16[64,16,202]{2,1,0:T(8,128)(2,1)} %constant_dynamic-slice_fusion), channel_id=1, source_target_pairs={{28,0},{0,4},{4,8},{8,12},{12,16},{16,20},{20,24},{24,28},{29,1},{... | collective-permute-start | bytes 1241096 | tf_op jit(solution)/shard_map/ppermute | solution.py:17
  64.5 25.9 %collective-permute-start.1 = (bf16[64,16,202]{2,1,0:T(8,128)(2,1)}, bf16[64,16,202]{2,1,0:T(8,128)(2,1)}, u32[]{:S(2)}, u32[]{:S(2)}) collective-permute-start(bf16[64,16,202]{2,1,0:T(8,128)(2,1)} %constant_dynamic-slice_fusion), channel_id=1, source_target_pairs={{24,0},{28,4},{0,8},{4,12},{8,16},{12,20},{16,24},{20,28},{25,1},{... | collective-permute-start | bytes 1241096 | tf_op jit(solution)/shard_map/ppermute | solution.py:17
Sparse Core Ops, SparseCore 0:
  39.5 21.6 all-gather.1
where the time goes:
time: 118 us; the launch traced here: 117 us
  waiting for transfers between devices  33.2 us (28%)
  local copies, waits for them, and re-layouts  27 us (23%)
  blocking collectives  20.1 us (17%)
  between operations  13.5 us (11%)
  other arithmetic  11.1 us (9%)
  matrix products  9.09 us (8%)
  starting transfers between devices  2.96 us (3%)
    all_gather x1, waiting for transfers between devices, on_device_local(): gathered = lax.all_gather(own, 'tm', axis=0, tiled=True)  21.7 us
    all_to_all x1, blocking collectives, on_device_local(): lax.all_to_all(spectra, 'chan', split_axis=1, concat_axis=0, tiled=True)  20.1 us
    ppermute x2, waiting for transfers between devices, shifted(): return lax.ppermute(block, axis, route)  11.4 us
    reshape x2, local copies, waits for them, and re-layouts, on_device_local(): own_spec = gathered.reshape(windows_all, block_width, 2, FB)  10.8 us
    reshape x2, local copies, waits for them, and re-layouts, on_device_local(): jnp.concatenate(partners, axis=1)  6.96 us
    dot_general x1, matrix products, on_device_local(): jnp.einsum('wicf,wjcf->fji', partner, both, preferred_element_type=jnp.fl...  5.77 us
    ppermute x2, starting transfers between devices, shifted(): return lax.ppermute(block, axis, route)  2.96 us
    gather x1, local copies, waits for them, and re-layouts, on_device_local(): spectra = jnp.take(spectra, chan_order, axis=1)  2.57 us
  transfers between devices with their start and end apart: 3, of which 2 were waited for; matrix products, arithmetic and copies ran while one was open for 11% of the time, Pallas kernels for 0%

commit v1 on v0

--- a/solution.py
+++ b/solution.py
@@ -102,7 +102,9 @@
     windows = records.reshape(samples // L, L, channels)
     spectra = whiten_spectra(windows, live_mask, precision=lax.Precision.HIGH)
     spectra = jnp.take(spectra, chan_order, axis=1)
-    own = lax.all_to_all(spectra, "chan", split_axis=1, concat_axis=0, tiled=True)
+    own = jnp.concatenate(
+        lax.all_to_all(jnp.stack(jnp.split(spectra, lax.axis_size("chan"), 1), 0), "chan", 0, 0), 0
+    )
     gathered = lax.all_gather(own, "tm", axis=0, tiled=True)
     windows_all = gathered.shape[0]
     own_spec = gathered.reshape(windows_all, block_width, 2, FB)

time: 118 us -> 118 us (level)
  no operation moved by 1% of the time
where the time goes in v1:
time: 118 us; the launch traced here: 117 us
  waiting for transfers between devices  33.2 us (28%)
  local copies, waits for them, and re-layouts  27.5 us (23%)
  blocking collectives  20.1 us (17%)
  between operations  13.6 us (12%)
  other arithmetic  11.1 us (9%)
  matrix products  9.09 us (8%)
  starting transfers between devices  2.96 us (3%)
    all_gather x1, waiting for transfers between devices, on_device_local(): gathered = lax.all_gather(own, 'tm', axis=0, tiled=True)  21.7 us
    all_to_all x1, blocking collectives, on_device_local(): lax.all_to_all(jnp.stack(jnp.split(spectra, lax.axis_size('chan'), 1), 0)...  20.1 us
    ppermute x2, waiting for transfers between devices, shifted(): return lax.ppermute(block, axis, route)  11.4 us
    reshape x2, local copies, waits for them, and re-layouts, on_device_local(): own_spec = gathered.reshape(windows_all, block_width, 2, FB)  10.8 us
    reshape x2, local copies, waits for them, and re-layouts, on_device_local(): jnp.concatenate(partners, axis=1)  6.96 us
    dot_general x1, matrix products, on_device_local(): jnp.einsum('wicf,wjcf->fji', partner, both, preferred_element_type=jnp.fl...  5.77 us
    ppermute x2, starting transfers between devices, shifted(): return lax.ppermute(block, axis, route)  2.96 us
    gather x1, local copies, waits for them, and re-layouts, on_device_local(): spectra = jnp.take(spectra, chan_order, axis=1)  2.57 us
  transfers between devices with their start and end apart: 3, of which 2 were waited for; matrix products, arithmetic and copies ran while one was open for 11% of the time, Pallas kernels for 0%

profile of v1, /device:TPU:4, one launch (start us, length us, event | category | flops | bytes accessed | tf_op | source)
XLA Modules:
  0.0 117.4 jit_solution(7977693875803705047)
XLA Ops:
  6.5 0.0 all-gather.2.cloned.1.call-start
  6.5 0.4 sine_negate_fusion
  7.0 0.1 convert_reduce_fusion
  7.1 0.7 compare_select_fusion
  7.8 0.7 compare_and_fusion
  8.5 1.2 %reduce_sum.36 = f32[2,512]{1,0:T(2,128)S(1)} reduce(f32[2,200,512]{2,1,0:T(8,128)} %bitcast.62, f32[]{:T(128)} %constant.41.clone.1), dimensions={1}, to_apply=%region_0.0 | reduce | flops 203776 | bytes 823300 | tf_op jit(solution)/shard_map/reduce_sum | solution.py:47
  9.7 1.3 %multiply_reduce_fusion = f32[2,512]{1,0:T(2,128)S(1)} fusion(f32[2,200,512]{2,1,0:T(8,128)} %bitcast.63, f32[2,512]{1,0:T(2,128)S(1)} %broadcast_multiply_fusion.1), kind=kLoop, calls=%fused_computation.18 | loop fusion | flops 613376 | bytes 827392 | tf_op jit(solution)/shard_map/reduce_sum | solution.py:49
  11.0 0.0 copy-start
  11.0 1.8 %fusion.12 = f32[2,512,202]{1,2,0:T(8,128)S(1)} fusion(f32[2,200,512]{2,1,0:T(8,128)} %bitcast.64, f32[2,512]{1,0:T(2,128)S(1)} %add_sqrt_fusion, f32[2,512]{1,0:T(2,128)S(1)} %broadcast_multiply_fusion.1, f32[200,101]{1,0:T(8,128)S(1)} %get-tuple-element.11, f32[200,101]{1,0:T(8,128)S(1)} %get-tuple-element.12), kind=kOutput, calls=%fused_computation.16 | convolution fusion | flops 248667600 | bytes 1816384 | tf_op jit(solution)/shard_map/...lk,lg->...kg/dot_general | solution.py:50
  12.8 0.1 fusion.28
  12.9 0.0 copy-done
  12.9 0.5 multiply_convert_fusion.1
  13.4 0.1 pad_maximum_fusion.1
  13.5 0.4 copy.23
  14.0 2.6 %gather_fusion = bf16[512,2,202]{2,1,0:T(2,128)(2,1)S(1)} fusion(bf16[2,512,202]{2,0,1:T(2,128)(2,1)S(1)} %copy.23, s32[1024]{0:T(1024)S(1)} %pad_clamp_fusion), kind=kCustom, calls=%fused_computation | custom fusion | bytes 829440 | tf_op jit(solution)/shard_map/jit(_take)/gather | solution.py:104
  16.5 1.8 %fusion.15 = bf16[2,512,202]{2,0,1:T(2,128)(2,1)S(1)} fusion(bf16[512,2,202]{2,1,0:T(2,128)(2,1)S(1)} %gather_fusion, pred[512]{0:T(512)(128)(4,1)S(1)} %compare_and_fusion), kind=kLoop, calls=%fused_computation.20 | loop fusion | flops 206848 | bytes 827904 | tf_op jit(solution)/shard_map/jit(_take)/select_n | solution.py:104
  18.4 0.1 fusion.35
  18.5 0.1 fusion.34
  18.5 0.1 fusion.33
  18.6 0.1 fusion.32
  18.7 0.1 fusion.31
  18.7 0.1 fusion.30
  18.8 0.1 fusion.29
  18.8 20.1 %all_to_all.5 = bf16[8,2,64,202]{3,1,2,0:T(2,128)(2,1)S(1)} all-to-all(bf16[8,2,64,202]{3,1,2,0:T(2,128)(2,1)S(1)} %fusion.29), channel_id=1, replica_groups=mesh['chan'=8,'tm'=4] {'chan'}, dimensions={0} | all-to-all | bytes 827392 | tf_op jit(solution)/shard_map/all_to_all | solution.py:106
  38.9 0.9 copy.24
  39.8 0.0 all-gather.2.cloned.1.call-update
  39.8 21.7 %all-gather.2.cloned.1.call-done = bf16[64,64,202]{2,1,0:T(8,128)(2,1)} async-done(((bf16[16,64,202]{2,1,0:T(8,128)(2,1)}), bf16[64,64,202]{2,1,0:T(8,128)(2,1)}) %all-gather.2.cloned.1.call-update) | async-done | bytes 1654800 | tf_op jit(solution)/shard_map/all_gather | solution.py:108
  61.6 1.9 %constant_dynamic-slice_fusion = bf16[64,16,202]{2,1,0:T(8,128)(2,1)} fusion(bf16[64,64,202]{2,1,0:T(8,128)(2,1)} %all-gather.2.cloned.1.call-done, s32[]{:T(128)S(6)} %select_n.58), kind=kLoop, calls=%fused_computation.83 | loop fusion | bytes 827396 | tf_op jit(solution)/shard_map/dynamic_slice | solution.py:113
  63.5 1.5 %collective-permute-start = (bf16[64,16,202]{2,1,0:T(8,128)(2,1)}, bf16[64,16,202]{2,1,0:T(8,128)(2,1)}, u32[]{:S(2)}, u32[]{:S(2)}) collective-permute-start(bf16[64,16,202]{2,1,0:T(8,128)(2,1)} %constant_dynamic-slice_fusion), channel_id=1, source_target_pairs={{28,0},{0,4},{4,8},{8,12},{12,16},{16,20},{20,24},{24,28},{29,1},{... | collective-permute-start | bytes 1241096 | tf_op jit(solution)/shard_map/ppermute | solution.py:17
  64.9 1.5 %collective-permute-start.1 = (bf16[64,16,202]{2,1,0:T(8,128)(2,1)}, bf16[64,16,202]{2,1,0:T(8,128)(2,1)}, u32[]{:S(2)}, u32[]{:S(2)}) collective-permute-start(bf16[64,16,202]{2,1,0:T(8,128)(2,1)} %constant_dynamic-slice_fusion), channel_id=1, source_target_pairs={{24,0},{28,4},{0,8},{4,12},{8,16},{12,20},{16,24},{20,28},{25,1},{... | collective-permute-start | bytes 1241096 | tf_op jit(solution)/shard_map/ppermute | solution.py:17
  66.4 0.2 cosine_multiply_fusion
  66.7 4.3 %reshape.189 = bf16[64,64,2,101]{3,2,1,0:T(2,128)(2,1)} reshape(bf16[64,64,202]{2,1,0:T(8,128)(2,1)} %all-gather.2.cloned.1.call-done) | data formatting | bytes 3309568 | tf_op jit(solution)/shard_map/reshape | solution.py:110
  71.0 6.4 %copy.27 = bf16[64,64,2,101]{1,0,2,3:T(8,128)(2,1)S(1)} copy(bf16[64,64,2,101]{3,2,1,0:T(2,128)(2,1)} %reshape.189) | data formatting | bytes 3309568 | tf_op jit(solution)/shard_map/reshape | solution.py:110
  77.4 2.0 %fusion.52 = (bf16[64,64,1,101]{1,0,2,3:T(8,128)(2,1)}, bf16[64,64,1,101]{1,0,2,3:T(8,128)(2,1)}) fusion(bf16[64,64,2,101]{1,0,2,3:T(8,128)(2,1)S(1)} %copy.27), kind=kLoop, calls=%fused_computation.89 | loop fusion | flops 413696 | bytes 3309568 | tf_op jit(solution)/shard_map/slice | solution.py:111
  79.4 0.0 collective-permute-done
  79.4 11.4 %collective-permute-done.1 = bf16[64,16,202]{2,1,0:T(8,128)(2,1)} collective-permute-done((bf16[64,16,202]{2,1,0:T(8,128)(2,1)}, bf16[64,16,202]{2,1,0:T(8,128)(2,1)}, u32[]{:S(2)}, u32[]{:S(2)}) %collective-permute-start.1) | collective-permute-done | bytes 413728 | tf_op jit(solution)/shard_map/ppermute | solution.py:17
  90.9 2.4 %pad_maximum_fusion = bf16[64,32,202]{2,1,0:T(8,128)(2,1)} fusion(bf16[64,16,202]{2,1,0:T(8,128)(2,1)} %collective-permute-done.1, bf16[64,16,202]{2,1,0:T(8,128)(2,1)} %collective-permute-done), kind=kLoop, calls=%fused_computation.14 | loop fusion | flops 1654784 | bytes 1654784 | tf_op jit(solution)/shard_map/concatenate | solution.py:118
  93.3 2.5 %reshape.190 = bf16[64,32,2,101]{3,2,1,0:T(2,128)(2,1)} reshape(bf16[64,32,202]{2,1,0:T(8,128)(2,1)} %pad_maximum_fusion) | data formatting | bytes 1654784 | tf_op jit(solution)/shard_map/reshape | solution.py:118
  95.8 4.5 %copy.28 = bf16[64,32,2,101]{0,1,2,3:T(8,128)(2,1)} copy(bf16[64,32,2,101]{3,2,1,0:T(2,128)(2,1)} %reshape.190) | data formatting | bytes 1654784 | tf_op jit(solution)/shard_map/reshape | solution.py:118
  100.3 5.8 %fusion.6 = f32[101,128,32]{1,2,0:T(8,128)} fusion(bf16[64,32,2,101]{0,1,2,3:T(8,128)(2,1)} %copy.28, bf16[64,64,1,101]{1,0,2,3:T(8,128)(2,1)} %get-tuple-element.6, bf16[64,64,1,101]{1,0,2,3:T(8,128)(2,1)} %get-tuple-element.5, bf16[64,64,2,101]{1,0,2,3:T(8,128)(2,1)S(1)} %copy.27), kind=kOutput, calls=%fused_computation.8 | convolution fusion | flops 115834880 | bytes 5791744 | tf_op jit(solution)/shard_map/wicf,wjcf->fji/dot_general | solution.py:119
  106.0 1.9 %copy.35 = f32[101,128,32]{0,1,2:T(8,128)S(1)} copy(f32[101,128,32]{1,2,0:T(8,128)} %fusion.6) | data formatting | bytes 3309568 | tf_op jit(solution)/shard_map/reshape | solution.py:120
  108.0 1.0 convolution_bitcast_fusion
  109.0 1.6 %copy.31 = f32[2,64,16,128]{3,2,1,0:T(8,128)} copy(f32[2,64,16,128]{3,1,2,0:T(8,128)S(1)} %convolution_bitcast_fusion) | data formatting | bytes 2097152 | tf_op jit(solution)/shard_map/fcjri,cfl->rjil/transpose | solution.py:121
  (8 shorter events, 0.1 us)
Async XLA Ops:
  6.5 55.0 %all-gather.2.cloned.1.call-start = ((), (), s32[]{:S(2)}) async-start(), calls=%async_computation.1 | async-start | bytes 2621440 | tf_op jit(solution)/shard_map/all_gather | solution.py:108
  11.0 1.9 %copy-start = (s32[512]{0:T(512)S(1)}, s32[512]{0:T(512)}, u32[]{:S(2)}) copy-start(s32[512]{0:T(512)} %param.5) | copy-start | bytes 6148
  63.5 16.0 %collective-permute-start = (bf16[64,16,202]{2,1,0:T(8,128)(2,1)}, bf16[64,16,202]{2,1,0:T(8,128)(2,1)}, u32[]{:S(2)}, u32[]{:S(2)}) collective-permute-start(bf16[64,16,202]{2,1,0:T(8,128)(2,1)} %constant_dynamic-slice_fusion), channel_id=1, source_target_pairs={{28,0},{0,4},{4,8},{8,12},{12,16},{16,20},{20,24},{24,28},{29,1},{... | collective-permute-start | bytes 1241096 | tf_op jit(solution)/shard_map/ppermute | solution.py:17
  64.9 25.9 %collective-permute-start.1 = (bf16[64,16,202]{2,1,0:T(8,128)(2,1)}, bf16[64,16,202]{2,1,0:T(8,128)(2,1)}, u32[]{:S(2)}, u32[]{:S(2)}) collective-permute-start(bf16[64,16,202]{2,1,0:T(8,128)(2,1)} %constant_dynamic-slice_fusion), channel_id=1, source_target_pairs={{24,0},{28,4},{0,8},{4,12},{8,16},{12,20},{16,24},{20,28},{25,1},{... | collective-permute-start | bytes 1241096 | tf_op jit(solution)/shard_map/ppermute | solution.py:17
Sparse Core Ops, SparseCore 0:
  39.9 21.6 all-gather.1
